TPU v7x, 512 devices: a whole 4x8x8 slice. The times are simulated.
512 devices in a mesh: param: 32 (over x, z), ex: 16 (over y, core).
Axes of the slice: x: 4, y: 8, z: 8, core: 2. Of those that a mesh axis runs over, the one named last changes fastest.
Arguments:
- adapter_gradients: bfloat16 [512, 131072], P('ex', 'param'), may hold values from -560 to 560
- sign_hash_keys: int32 [4], replicated, may hold values from 1 to 16777215
- target_indices: int32 [256], replicated, may hold values from 0 to 511
Outputs:
- features: float32 [512, 8192], P('ex', 'param')
- scores: float32 [512, 256], P('ex')
All inputs are finite; a program needn't handle non-finite values.
Results may differ from a plain program's by a relative error of at most 0.0003.
Values sent between devices are 32-bit elements; how exact they have to be, the bound alone decides.
No kernel may reach another device: no remote copies, remote signals or barrier semaphores. Data moves between devices by JAX's collectives and lax.ppermute only.
A program may use at most 128 MiB of HBM per device.

v0:
```python
import jax
import jax.numpy as jnp
from jax import lax
from jax.sharding import Mesh, PartitionSpec as P

K = 8192
norm_eps = 1e-06


def hash_terms(sign_hash_keys, first_row, row_count, col_ids):
    mult_row = sign_hash_keys[0] | 1
    mult_col = sign_hash_keys[1] | 1
    seed_add = sign_hash_keys[2]
    row_ids = first_row + lax.iota(jnp.int32, row_count)
    return (row_ids * mult_row + seed_add, col_ids * mult_col)


def sign_block(sign_hash_keys, row_terms, col_terms):
    mix_mult = sign_hash_keys[3] | 1
    hashed = row_terms[:, None] + col_terms[None, :]
    hashed = hashed ^ lax.shift_right_logical(hashed, jnp.full_like(hashed, 16))
    hashed = hashed * mix_mult
    hashed = hashed ^ lax.shift_right_logical(hashed, jnp.full_like(hashed, 13))
    hashed = hashed * jnp.int32(-1028477387)
    hashed = hashed ^ lax.shift_right_logical(hashed, jnp.full_like(hashed, 16))
    return jnp.where(hashed < 0, jnp.bfloat16(1.0), jnp.bfloat16(-1.0))


def butterfly_sum(values, axis, count):
    distance = 1
    while distance < count:
        pairs = [(j, j ^ distance) for j in range(count)]
        values = values + lax.ppermute(values, axis, pairs)
        distance *= 2
    return values


def local(adapter_gradients, sign_hash_keys, target_indices):
    resident_example, resident_rows = adapter_gradients.shape
    row_base = lax.axis_index("param") * jnp.int32(resident_rows)
    core = lax.axis_index("ec")
    swap = [(0, 1), (1, 0)]
    turn_count = 2
    rows_per_tile = resident_rows // turn_count
    scale_k = jnp.float32(K)
    param_count = lax.psum(1, "param")
    col_width = K // param_count
    half_width = col_width // 2
    unit = ((sign_hash_keys[3] | 1) & 1).astype(jnp.float32)
    partner = lax.ppermute(adapter_gradients.astype(jnp.float32), "ec", swap) * unit
    partner = partner.astype(jnp.bfloat16)
    pair_gradients = jnp.where(
        core == 0,
        jnp.concatenate([adapter_gradients, partner], axis=0),
        jnp.concatenate([partner, adapter_gradients], axis=0),
    )
    owner = lax.iota(jnp.int32, param_count)[:, None] * col_width
    col_ids = (owner + core * half_width + lax.iota(jnp.int32, half_width)[None, :]).reshape(-1)
    row_terms, col_terms = hash_terms(sign_hash_keys, row_base, resident_rows, col_ids)
    totals = None
    for tile in range(turn_count):
        start_offset = tile * rows_per_tile
        gradient_slab = pair_gradients[:, start_offset : start_offset + rows_per_tile]
        signs = sign_block(
            sign_hash_keys, row_terms[start_offset : start_offset + rows_per_tile], col_terms
        )
        term = jnp.einsum(
            "cra,apj->pcrj",
            gradient_slab.reshape(2, resident_example, rows_per_tile),
            signs.reshape(rows_per_tile, param_count, half_width),
            preferred_element_type=jnp.float32,
        )
        totals = term if totals is None else totals + term
    blocks = totals.reshape(2 * param_count, resident_example, half_width)
    blocks = lax.all_to_all(blocks, ("param", "ec"), 0, 0, tiled=True)
    blocks = jnp.sum(blocks.reshape(param_count, 2, resident_example, half_width), axis=0)
    projected = jnp.transpose(blocks, (1, 0, 2)).reshape(resident_example, col_width)
    pool_rows = lax.all_gather(projected, ("ey", "ec"), axis=0, tiled=True)
    picks = (target_indices[:, None] == lax.iota(jnp.int32, pool_rows.shape[0])[None, :]).astype(
        jnp.float32
    )
    target_rows = jnp.dot(picks, pool_rows, precision=lax.Precision.HIGHEST)
    partial_dots = jnp.dot(projected, target_rows.T, precision=lax.Precision.HIGHEST)
    own_squares = jnp.sum(projected * projected, axis=1)
    target_squares = jnp.sum(target_rows * target_rows, axis=1)
    packed = jnp.concatenate([partial_dots.reshape(-1), own_squares, target_squares])
    packed = butterfly_sum(packed, "param", param_count)
    dot_count = partial_dots.size
    dots = packed[:dot_count].reshape(partial_dots.shape)
    total_sq = packed[dot_count : dot_count + resident_example]
    target_sq = packed[dot_count + resident_example :]
    own_scale = jnp.sqrt(scale_k / (total_sq + norm_eps))
    target_scale = jnp.sqrt(scale_k / (target_sq + norm_eps))
    features = projected * own_scale[:, None]
    scores = dots * own_scale[:, None] * target_scale[None, :] / scale_k
    return (features, scores)


def solution(mesh):
    devices = mesh.devices
    pair_mesh = Mesh(
        devices.reshape(devices.shape[0], devices.shape[1] // 2, 2), ("param", "ey", "ec")
    )
    return jax.shard_map(
        local,
        mesh=pair_mesh,
        in_specs=(P(("ey", "ec"), "param"), P(), P()),
        out_specs=(P(("ey", "ec"), "param"), P(("ey", "ec"), None)),
        check_vma=False,
    )
```

profile of v0, /device:TPU:2, one launch (start us, length us, event | category | flops | bytes accessed | tf_op | source)
XLA Modules:
  0.0 132.4 jit_solution(819672193502317939)
XLA Ops:
  0.6 0.0 copy-start
  0.6 1.1 convert_element_type.10
  1.7 1.9 %collective-permute-start = (f32[32,4096]{1,0:T(8,128)S(1)}, f32[32,4096]{1,0:T(8,128)S(1)}, u32[]{:S(2)}, u32[]{:S(2)}) collective-permute-start(f32[32,4096]{1,0:T(8,128)S(1)} %convert_element_type.10), channel_id=1, source_target_pairs={{0,1},{1,0},{2,3},{3,2},{4,5},{5,4},{6,7},{7,6},{8,9},{9,8},{10,11... | collective-permute-start | bytes 1572872 | tf_op jit(solution)/shard_map/ppermute | solution.py:50
  3.6 1.5 %fusion.42 = (s32[1]{0:T(128)}, s32[1]{0:T(128)}, s32[1]{0:T(128)}, s32[1]{0:T(128)}) fusion(s32[4]{0:T(128)} %param.4), kind=kLoop, calls=%fused_computation.58 | loop fusion | bytes 32 | tf_op jit(solution)/shard_map/slice | solution.py:12
  7.0 0.7 multiply_add_fusion
  7.7 0.1 add_multiply_fusion
  7.8 0.0 collective-permute-done
  7.8 0.0 copy-done
  7.8 0.1 maximum_select_fusion
  8.0 13.4 %fusion.10 = f32[32,128,2,32]{1,3,2,0:T(8,128)S(1)} fusion(bf16[2,32,2048,1]{2,1,0,3:T(8,128)(2,1)S(1)} %bitcast.53, s32[2048]{0:T(1024)S(1)} %get-tuple-element.5, s32[]{:T(128)} %bitcast.3, s32[32,128]{1,0:T(8,128)S(1)} %add_multiply_fusion), kind=kOutput, calls=%fused_computation.16 | convolution fusion | flops 1166016512 | bytes 1335300 | tf_op jit(solution)/shard_map/cra,apj->pcrj/dot_general | solution.py:67
  21.4 13.5 %fusion.18 = f32[32,128,2,32]{1,3,2,0:T(8,128)S(1)} fusion(f32[32,128,2,32]{1,3,2,0:T(8,128)S(1)} %fusion.10, bf16[2,32,2048,1]{2,1,0,3:T(8,128)(2,1)S(1)} %bitcast.52, s32[]{:T(128)} %bitcast.3, s32[32,128]{1,0:T(8,128)S(1)} %add_multiply_fusion, s32[2048]{0:T(1024)S(1)} %get-tuple-element.4), kind=kOutput, calls=%fused_computation.22 | convolution fusion | flops 1166278656 | bytes 2383876 | tf_op jit(solution)/shard_map/cra,apj->pcrj/dot_general | solution.py:67
  34.9 40.9 %all_to_all.5 = f32[64,32,128]{2,1,0:T(8,128)S(1)} all-to-all(f32[64,32,128]{2,1,0:T(8,128)S(1)} %bitcast.51), channel_id=1, replica_groups=mesh['param'=32,'ey'=8,'ec'=2] {'param','ec'}, dimensions={0} | all-to-all | bytes 2097152 | tf_op jit(solution)/shard_map/all_to_all | solution.py:75
  75.8 0.0 copy-start.1
  75.8 0.1 reduce_sum.27
  75.9 0.1 fusion.23
  76.0 19.0 %all_gather.3 = f32[512,256]{1,0:T(8,128)S(1)} all-gather(f32[32,256]{1,0:T(8,128)S(1)} %copy_bitcast_fusion), channel_id=1, replica_groups=mesh['param'=32,'ey'=8,'ec'=2] {'ey','ec'}, dimensions={0}, use_global_device_ids=true | all-gather | bytes 557056 | tf_op jit(solution)/shard_map/all_gather | solution.py:78
  95.0 0.0 copy-done.1
  95.0 0.7 multiply_reduce_fusion
  95.7 0.2 convolution_bitcast_fusion
  96.0 0.1 concatenate.11
  96.1 3.3 %collective-permute-start.1 = (f32[8480]{0:T(1024)S(1)}, f32[8480]{0:T(1024)S(1)}, u32[]{:S(2)}, u32[]{:S(2)}) collective-permute-start(f32[8480]{0:T(1024)S(1)} %concatenate.11), channel_id=1, source_target_pairs={{0,16},{16,0},{32,48},{48,32},{64,80},{80,64},{96,112},{112,96},{1... | collective-permute-start | bytes 101768 | tf_op jit(solution)/shard_map/ppermute | solution.py:33
  99.3 2.6 %collective-permute-done.1 = f32[8480]{0:T(1024)S(1)} collective-permute-done((f32[8480]{0:T(1024)S(1)}, f32[8480]{0:T(1024)S(1)}, u32[]{:S(2)}, u32[]{:S(2)}) %collective-permute-start.1) | collective-permute-done | bytes 33952 | tf_op jit(solution)/shard_map/ppermute | solution.py:33
  101.9 4.8 %collective-permute-start.2 = (f32[8480]{0:T(1024)S(1)}, f32[8480]{0:T(1024)S(1)}, u32[]{:S(2)}, u32[]{:S(2)}) collective-permute-start(f32[8480]{0:T(1024)S(1)} %add.124), channel_id=1, source_target_pairs={{0,32},{16,48},{32,0},{48,16},{64,96},{80,112},{96,64},{112,80},{1... | collective-permute-start | bytes 101768 | tf_op jit(solution)/shard_map/ppermute | solution.py:33
  106.7 1.9 %collective-permute-done.2 = f32[8480]{0:T(1024)S(1)} collective-permute-done((f32[8480]{0:T(1024)S(1)}, f32[8480]{0:T(1024)S(1)}, u32[]{:S(2)}, u32[]{:S(2)}) %collective-permute-start.2) | collective-permute-done | bytes 33952 | tf_op jit(solution)/shard_map/ppermute | solution.py:33
  108.7 5.2 %collective-permute-start.3 = (f32[8480]{0:T(1024)S(1)}, f32[8480]{0:T(1024)S(1)}, u32[]{:S(2)}, u32[]{:S(2)}) collective-permute-start(f32[8480]{0:T(1024)S(1)} %add.125), channel_id=1, source_target_pairs={{0,64},{16,80},{32,96},{48,112},{64,0},{80,16},{96,32},{112,48},{1... | collective-permute-start | bytes 101768 | tf_op jit(solution)/shard_map/ppermute | solution.py:33
  113.9 4.5 %collective-permute-done.3 = f32[8480]{0:T(1024)S(1)} collective-permute-done((f32[8480]{0:T(1024)S(1)}, f32[8480]{0:T(1024)S(1)}, u32[]{:S(2)}, u32[]{:S(2)}) %collective-permute-start.3) | collective-permute-done | bytes 33952 | tf_op jit(solution)/shard_map/ppermute | solution.py:33
  118.4 3.4 %collective-permute-start.4 = (f32[8480]{0:T(1024)S(1)}, f32[8480]{0:T(1024)S(1)}, u32[]{:S(2)}, u32[]{:S(2)}) collective-permute-start(f32[8480]{0:T(1024)S(1)} %add.126), channel_id=1, source_target_pairs={{0,128},{16,144},{32,160},{48,176},{64,192},{80,208},{96,224},{112... | collective-permute-start | bytes 101768 | tf_op jit(solution)/shard_map/ppermute | solution.py:33
  121.9 2.4 %collective-permute-done.4 = f32[8480]{0:T(1024)S(1)} collective-permute-done((f32[8480]{0:T(1024)S(1)}, f32[8480]{0:T(1024)S(1)}, u32[]{:S(2)}, u32[]{:S(2)}) %collective-permute-start.4) | collective-permute-done | bytes 33952 | tf_op jit(solution)/shard_map/ppermute | solution.py:33
  124.3 4.0 %collective-permute-start.5 = (f32[8480]{0:T(1024)S(1)}, f32[8480]{0:T(1024)S(1)}, u32[]{:S(2)}, u32[]{:S(2)}) collective-permute-start(f32[8480]{0:T(1024)S(1)} %add.127), channel_id=1, source_target_pairs={{0,256},{16,272},{32,288},{48,304},{64,320},{80,336},{96,352},{112... | collective-permute-start | bytes 101768 | tf_op jit(solution)/shard_map/ppermute | solution.py:33
  128.3 3.3 %collective-permute-done.5 = f32[8480]{0:T(1024)S(1)} collective-permute-done((f32[8480]{0:T(1024)S(1)}, f32[8480]{0:T(1024)S(1)}, u32[]{:S(2)}, u32[]{:S(2)}) %collective-permute-start.5) | collective-permute-done | bytes 33952 | tf_op jit(solution)/shard_map/ppermute | solution.py:33
  131.6 0.1 fusion.25
  131.7 0.7 multiply_multiply_fusion
  (14 shorter events, 0.2 us)
Async XLA Ops:
  0.6 7.2 %copy-start = (bf16[32,4096]{1,0:T(8,128)(2,1)S(1)}, bf16[32,4096]{1,0:T(8,128)(2,1)}, u32[]{:S(2)}) copy-start(bf16[32,4096]{1,0:T(8,128)(2,1)} %param.3) | copy-start | bytes 786436
  1.7 6.1 %collective-permute-start = (f32[32,4096]{1,0:T(8,128)S(1)}, f32[32,4096]{1,0:T(8,128)S(1)}, u32[]{:S(2)}, u32[]{:S(2)}) collective-permute-start(f32[32,4096]{1,0:T(8,128)S(1)} %convert_element_type.10), channel_id=1, source_target_pairs={{0,1},{1,0},{2,3},{3,2},{4,5},{5,4},{6,7},{7,6},{8,9},{9,8},{10,11... | collective-permute-start | bytes 1572872 | tf_op jit(solution)/shard_map/ppermute | solution.py:50
  75.8 19.2 %copy-start.1 = (s32[256]{0:T(256)S(1)}, s32[256]{0:T(256)}, u32[]{:S(2)}) copy-start(s32[256]{0:T(256)} %param.5) | copy-start | bytes 3076
  96.1 5.8 %collective-permute-start.1 = (f32[8480]{0:T(1024)S(1)}, f32[8480]{0:T(1024)S(1)}, u32[]{:S(2)}, u32[]{:S(2)}) collective-permute-start(f32[8480]{0:T(1024)S(1)} %concatenate.11), channel_id=1, source_target_pairs={{0,16},{16,0},{32,48},{48,32},{64,80},{80,64},{96,112},{112,96},{1... | collective-permute-start | bytes 101768 | tf_op jit(solution)/shard_map/ppermute | solution.py:33
  101.9 6.7 %collective-permute-start.2 = (f32[8480]{0:T(1024)S(1)}, f32[8480]{0:T(1024)S(1)}, u32[]{:S(2)}, u32[]{:S(2)}) collective-permute-start(f32[8480]{0:T(1024)S(1)} %add.124), channel_id=1, source_target_pairs={{0,32},{16,48},{32,0},{48,16},{64,96},{80,112},{96,64},{112,80},{1... | collective-permute-start | bytes 101768 | tf_op jit(solution)/shard_map/ppermute | solution.py:33
  108.7 9.7 %collective-permute-start.3 = (f32[8480]{0:T(1024)S(1)}, f32[8480]{0:T(1024)S(1)}, u32[]{:S(2)}, u32[]{:S(2)}) collective-permute-start(f32[8480]{0:T(1024)S(1)} %add.125), channel_id=1, source_target_pairs={{0,64},{16,80},{32,96},{48,112},{64,0},{80,16},{96,32},{112,48},{1... | collective-permute-start | bytes 101768 | tf_op jit(solution)/shard_map/ppermute | solution.py:33
  118.4 5.8 %collective-permute-start.4 = (f32[8480]{0:T(1024)S(1)}, f32[8480]{0:T(1024)S(1)}, u32[]{:S(2)}, u32[]{:S(2)}) collective-permute-start(f32[8480]{0:T(1024)S(1)} %add.126), channel_id=1, source_target_pairs={{0,128},{16,144},{32,160},{48,176},{64,192},{80,208},{96,224},{112... | collective-permute-start | bytes 101768 | tf_op jit(solution)/shard_map/ppermute | solution.py:33
  124.3 7.3 %collective-permute-start.5 = (f32[8480]{0:T(1024)S(1)}, f32[8480]{0:T(1024)S(1)}, u32[]{:S(2)}, u32[]{:S(2)}) collective-permute-start(f32[8480]{0:T(1024)S(1)} %add.127), channel_id=1, source_target_pairs={{0,256},{16,272},{32,288},{48,304},{64,320},{80,336},{96,352},{112... | collective-permute-start | bytes 101768 | tf_op jit(solution)/shard_map/ppermute | solution.py:33
where the time goes:
time: 133 us; the launch traced here: 132 us
  blocking collectives  59.9 us (45%)
  matrix products  27.9 us (21%)
  starting transfers between devices  22.7 us (17%)
  waiting for transfers between devices  14.7 us (11%)
  other arithmetic  2.91 us (2%)
  between operations  2.7 us (2%)
  local copies, waits for them, and re-layouts  1.65 us (1%)
    all_to_all x1, blocking collectives, local(): blocks = lax.all_to_all(blocks, ('param', 'ec'), 0, 0, tiled=True)  40.9 us
    dot_general x2, matrix products, local(): jnp.einsum('cra,apj->pcrj', gradient_slab.reshape(2, resident_example, ro...  27 us
    ppermute x5, starting transfers between devices, butterfly_sum(): values = values + lax.ppermute(values, axis, pairs)  20.8 us
    all_gather x1, blocking collectives, local(): pool_rows = lax.all_gather(projected, ('ey', 'ec'), axis=0, tiled=True)  19 us
    ppermute x5, waiting for transfers between devices, butterfly_sum(): values = values + lax.ppermute(values, axis, pairs)  14.7 us
  transfers between devices with their start and end apart: 6, of which 5 were waited for; matrix products, arithmetic and copies ran while one was open for 2% of the time, Pallas kernels for 0%

commit v1 on v0

--- a/solution.py
+++ b/solution.py
@@ -5,6 +5,11 @@
 
 K = 8192
 norm_eps = 1e-06
+
+
+def gather_over(x, name, dim):
+    sent = jnp.stack([x] * lax.axis_size(name))
+    return jnp.concatenate(lax.all_to_all(sent, name, 0, 0), axis=dim)
 
 
 def hash_terms(sign_hash_keys, first_row, row_count, col_ids):
@@ -75,7 +80,7 @@
     blocks = lax.all_to_all(blocks, ("param", "ec"), 0, 0, tiled=True)
     blocks = jnp.sum(blocks.reshape(param_count, 2, resident_example, half_width), axis=0)
     projected = jnp.transpose(blocks, (1, 0, 2)).reshape(resident_example, col_width)
-    pool_rows = lax.all_gather(projected, ("ey", "ec"), axis=0, tiled=True)
+    pool_rows = gather_over(projected, ("ey", "ec"), 0)
     picks = (target_indices[:, None] == lax.iota(jnp.int32, pool_rows.shape[0])[None, :]).astype(
         jnp.float32
     )

time: 133 us -> 140 us (1.053)
  waiting for transfers between devices: 14.7 us -> 36.2 us
  blocking collectives: 59.9 us -> 40.9 us
  starting transfers between devices: 22.7 us -> 26.5 us
    all_gather x1 -> x0, blocking collectives: 19 us -> none  [local(): pool_rows = lax.all_gather(projected, ('ey', 'ec'), axis=0, tiled=True)]
    all_to_all x0 -> x1, waiting for transfers between devices: none -> 15.9 us  [gather_over(): return jnp.concatenate(lax.all_to_all(sent, name, 0, 0), axis=dim)]
    all_to_all x0 -> x1, starting transfers between devices: none -> 8.22 us  [gather_over(): return jnp.concatenate(lax.all_to_all(sent, name, 0, 0), axis=dim)]
    ppermute x5, waiting for transfers between devices: 14.7 us -> 20.3 us  [butterfly_sum(): values = values + lax.ppermute(values, axis, pairs)]
    ppermute x5, starting transfers between devices: 20.8 us -> 16.4 us  [butterfly_sum(): values = values + lax.ppermute(values, axis, pairs)]
  transfers between devices with their start and end apart: 6 -> 7, of which waited for: 5 -> 6; matrix products, arithmetic and copies ran while one was open for 2% -> 2% of each run, Pallas kernels for 0% -> 0%
where the time goes in v1:
time: 140 us
  blocking collectives  40.9 us (29%)
  waiting for transfers between devices  36.2 us (26%)
  matrix products  27.9 us (20%)
  starting transfers between devices  26.5 us (19%)
  other arithmetic  2.91 us (2%)
  between operations  2.71 us (2%)
  local copies, waits for them, and re-layouts  2.48 us (2%)
    all_to_all x1, blocking collectives, local(): blocks = lax.all_to_all(blocks, ('param', 'ec'), 0, 0, tiled=True)  40.9 us
    dot_general x2, matrix products, local(): jnp.einsum('cra,apj->pcrj', gradient_slab.reshape(2, resident_example, ro...  27 us
    ppermute x5, waiting for transfers between devices, butterfly_sum(): values = values + lax.ppermute(values, axis, pairs)  20.3 us
    ppermute x5, starting transfers between devices, butterfly_sum(): values = values + lax.ppermute(values, axis, pairs)  16.4 us
    all_to_all x1, waiting for transfers between devices, gather_over(): return jnp.concatenate(lax.all_to_all(sent, name, 0, 0), axis=dim)  15.9 us
    all_to_all x1, starting transfers between devices, gather_over(): return jnp.concatenate(lax.all_to_all(sent, name, 0, 0), axis=dim)  8.22 us
  transfers between devices with their start and end apart: 7, of which 6 were waited for; matrix products, arithmetic and copies ran while one was open for 2% of the time, Pallas kernels for 0%

profile of v1, /device:TPU:2, one launch (start us, length us, event | category | flops | bytes accessed | tf_op | source)
XLA Modules:
  0.0 139.6 jit_solution(9576021797102325108)
XLA Ops:
  0.6 0.0 copy-start
  0.6 1.1 convert_element_type.10
  1.7 1.9 %collective-permute-start = (f32[32,4096]{1,0:T(8,128)S(1)}, f32[32,4096]{1,0:T(8,128)S(1)}, u32[]{:S(2)}, u32[]{:S(2)}) collective-permute-start(f32[32,4096]{1,0:T(8,128)S(1)} %convert_element_type.10), channel_id=1, source_target_pairs={{0,1},{1,0},{2,3},{3,2},{4,5},{5,4},{6,7},{7,6},{8,9},{9,8},{10,11... | collective-permute-start | bytes 1572872 | tf_op jit(solution)/shard_map/ppermute | solution.py:55
  3.6 1.5 %fusion.42 = (s32[1]{0:T(128)}, s32[1]{0:T(128)}, s32[1]{0:T(128)}, s32[1]{0:T(128)}) fusion(s32[4]{0:T(128)} %param.4), kind=kLoop, calls=%fused_computation.58 | loop fusion | bytes 32 | tf_op jit(solution)/shard_map/slice | solution.py:17
  7.0 0.7 multiply_add_fusion
  7.7 0.1 add_multiply_fusion
  7.7 0.0 collective-permute-done
  7.8 0.0 copy-done
  7.8 0.1 maximum_select_fusion
  7.9 13.4 %fusion.10 = f32[32,128,2,32]{1,3,2,0:T(8,128)S(1)} fusion(bf16[2,32,2048,1]{2,1,0,3:T(8,128)(2,1)S(1)} %bitcast.55, s32[2048]{0:T(1024)S(1)} %get-tuple-element.5, s32[]{:T(128)} %bitcast.3, s32[32,128]{1,0:T(8,128)S(1)} %add_multiply_fusion), kind=kOutput, calls=%fused_computation.16 | convolution fusion | flops 1166016512 | bytes 1335300 | tf_op jit(solution)/shard_map/cra,apj->pcrj/dot_general | solution.py:72
  21.4 13.5 %fusion.18 = f32[32,128,2,32]{1,3,2,0:T(8,128)S(1)} fusion(f32[32,128,2,32]{1,3,2,0:T(8,128)S(1)} %fusion.10, bf16[2,32,2048,1]{2,1,0,3:T(8,128)(2,1)S(1)} %bitcast.54, s32[]{:T(128)} %bitcast.3, s32[32,128]{1,0:T(8,128)S(1)} %add_multiply_fusion, s32[2048]{0:T(1024)S(1)} %get-tuple-element.4), kind=kOutput, calls=%fused_computation.22 | convolution fusion | flops 1166278656 | bytes 2383876 | tf_op jit(solution)/shard_map/cra,apj->pcrj/dot_general | solution.py:72
  34.9 40.9 %all_to_all.10 = f32[64,32,128]{2,1,0:T(8,128)S(1)} all-to-all(f32[64,32,128]{2,1,0:T(8,128)S(1)} %bitcast.53), channel_id=1, replica_groups=mesh['param'=32,'ey'=8,'ec'=2] {'param','ec'}, dimensions={0} | all-to-all | bytes 2097152 | tf_op jit(solution)/shard_map/all_to_all | solution.py:80
  75.8 0.1 reduce_sum.27
  75.9 0.0 copy-start.1
  75.9 0.8 stack.3
  76.7 8.2 %all-to-all-start.1 = ((f32[16,32,256]{2,1,0:T(8,128)}), f32[16,32,256]{2,1,0:T(8,128)S(1)}, u32[]{:S(2)}, u32[]{:S(2)}) async-start(f32[16,32,256]{2,1,0:T(8,128)} %stack.3), calls=%async_computation.1 | async-start | bytes 1048576 | tf_op jit(solution)/shard_map/all_to_all | solution.py:12
  85.0 0.1 fusion.23
  85.1 15.9 %all-to-all-done.1 = f32[16,32,256]{2,1,0:T(8,128)S(1)} async-done(((f32[16,32,256]{2,1,0:T(8,128)}), f32[16,32,256]{2,1,0:T(8,128)S(1)}, u32[]{:S(2)}, u32[]{:S(2)}) %all-to-all-start.1) | async-done | bytes 524320 | tf_op jit(solution)/shard_map/all_to_all | solution.py:12
  101.0 0.0 copy-done.1
  101.0 0.7 multiply_reduce_fusion
  101.7 0.2 convolution_bitcast_fusion
  101.9 0.1 concatenate.11
  102.0 2.5 %collective-permute-start.1 = (f32[8480]{0:T(1024)S(1)}, f32[8480]{0:T(1024)S(1)}, u32[]{:S(2)}, u32[]{:S(2)}) collective-permute-start(f32[8480]{0:T(1024)S(1)} %concatenate.11), channel_id=1, source_target_pairs={{0,16},{16,0},{32,48},{48,32},{64,80},{80,64},{96,112},{112,96},{1... | collective-permute-start | bytes 101768 | tf_op jit(solution)/shard_map/ppermute | solution.py:38
  104.5 3.4 %collective-permute-done.1 = f32[8480]{0:T(1024)S(1)} collective-permute-done((f32[8480]{0:T(1024)S(1)}, f32[8480]{0:T(1024)S(1)}, u32[]{:S(2)}, u32[]{:S(2)}) %collective-permute-start.1) | collective-permute-done | bytes 33952 | tf_op jit(solution)/shard_map/ppermute | solution.py:38
  107.9 3.8 %collective-permute-start.2 = (f32[8480]{0:T(1024)S(1)}, f32[8480]{0:T(1024)S(1)}, u32[]{:S(2)}, u32[]{:S(2)}) collective-permute-start(f32[8480]{0:T(1024)S(1)} %add.124), channel_id=1, source_target_pairs={{0,32},{16,48},{32,0},{48,16},{64,96},{80,112},{96,64},{112,80},{1... | collective-permute-start | bytes 101768 | tf_op jit(solution)/shard_map/ppermute | solution.py:38
  111.7 3.7 %collective-permute-done.2 = f32[8480]{0:T(1024)S(1)} collective-permute-done((f32[8480]{0:T(1024)S(1)}, f32[8480]{0:T(1024)S(1)}, u32[]{:S(2)}, u32[]{:S(2)}) %collective-permute-start.2) | collective-permute-done | bytes 33952 | tf_op jit(solution)/shard_map/ppermute | solution.py:38
  115.4 3.8 %collective-permute-start.3 = (f32[8480]{0:T(1024)S(1)}, f32[8480]{0:T(1024)S(1)}, u32[]{:S(2)}, u32[]{:S(2)}) collective-permute-start(f32[8480]{0:T(1024)S(1)} %add.125), channel_id=1, source_target_pairs={{0,64},{16,80},{32,96},{48,112},{64,0},{80,16},{96,32},{112,48},{1... | collective-permute-start | bytes 101768 | tf_op jit(solution)/shard_map/ppermute | solution.py:38
  119.2 6.3 %collective-permute-done.3 = f32[8480]{0:T(1024)S(1)} collective-permute-done((f32[8480]{0:T(1024)S(1)}, f32[8480]{0:T(1024)S(1)}, u32[]{:S(2)}, u32[]{:S(2)}) %collective-permute-start.3) | collective-permute-done | bytes 33952 | tf_op jit(solution)/shard_map/ppermute | solution.py:38
  125.5 2.5 %collective-permute-start.4 = (f32[8480]{0:T(1024)S(1)}, f32[8480]{0:T(1024)S(1)}, u32[]{:S(2)}, u32[]{:S(2)}) collective-permute-start(f32[8480]{0:T(1024)S(1)} %add.126), channel_id=1, source_target_pairs={{0,128},{16,144},{32,160},{48,176},{64,192},{80,208},{96,224},{112... | collective-permute-start | bytes 101768 | tf_op jit(solution)/shard_map/ppermute | solution.py:38
  128.0 3.4 %collective-permute-done.4 = f32[8480]{0:T(1024)S(1)} collective-permute-done((f32[8480]{0:T(1024)S(1)}, f32[8480]{0:T(1024)S(1)}, u32[]{:S(2)}, u32[]{:S(2)}) %collective-permute-start.4) | collective-permute-done | bytes 33952 | tf_op jit(solution)/shard_map/ppermute | solution.py:38
  131.4 3.8 %collective-permute-start.5 = (f32[8480]{0:T(1024)S(1)}, f32[8480]{0:T(1024)S(1)}, u32[]{:S(2)}, u32[]{:S(2)}) collective-permute-start(f32[8480]{0:T(1024)S(1)} %add.127), channel_id=1, source_target_pairs={{0,256},{16,272},{32,288},{48,304},{64,320},{80,336},{96,352},{112... | collective-permute-start | bytes 101768 | tf_op jit(solution)/shard_map/ppermute | solution.py:38
  135.2 3.5 %collective-permute-done.5 = f32[8480]{0:T(1024)S(1)} collective-permute-done((f32[8480]{0:T(1024)S(1)}, f32[8480]{0:T(1024)S(1)}, u32[]{:S(2)}, u32[]{:S(2)}) %collective-permute-start.5) | collective-permute-done | bytes 33952 | tf_op jit(solution)/shard_map/ppermute | solution.py:38
  138.7 0.1 fusion.25
  138.9 0.7 multiply_multiply_fusion
  (14 shorter events, 0.2 us)
Async XLA Ops:
  0.6 7.2 %copy-start = (bf16[32,4096]{1,0:T(8,128)(2,1)S(1)}, bf16[32,4096]{1,0:T(8,128)(2,1)}, u32[]{:S(2)}) copy-start(bf16[32,4096]{1,0:T(8,128)(2,1)} %param.3) | copy-start | bytes 786436
  1.7 6.1 %collective-permute-start = (f32[32,4096]{1,0:T(8,128)S(1)}, f32[32,4096]{1,0:T(8,128)S(1)}, u32[]{:S(2)}, u32[]{:S(2)}) collective-permute-start(f32[32,4096]{1,0:T(8,128)S(1)} %convert_element_type.10), channel_id=1, source_target_pairs={{0,1},{1,0},{2,3},{3,2},{4,5},{5,4},{6,7},{7,6},{8,9},{9,8},{10,11... | collective-permute-start | bytes 1572872 | tf_op jit(solution)/shard_map/ppermute | solution.py:55
  75.9 25.1 %copy-start.1 = (s32[256]{0:T(256)S(1)}, s32[256]{0:T(256)}, u32[]{:S(2)}) copy-start(s32[256]{0:T(256)} %param.5) | copy-start | bytes 3076
  76.7 24.3 %all-to-all-start.1 = ((f32[16,32,256]{2,1,0:T(8,128)}), f32[16,32,256]{2,1,0:T(8,128)S(1)}, u32[]{:S(2)}, u32[]{:S(2)}) async-start(f32[16,32,256]{2,1,0:T(8,128)} %stack.3), calls=%async_computation.1 | async-start | bytes 1048576 | tf_op jit(solution)/shard_map/all_to_all | solution.py:12
  102.0 5.8 %collective-permute-start.1 = (f32[8480]{0:T(1024)S(1)}, f32[8480]{0:T(1024)S(1)}, u32[]{:S(2)}, u32[]{:S(2)}) collective-permute-start(f32[8480]{0:T(1024)S(1)} %concatenate.11), channel_id=1, source_target_pairs={{0,16},{16,0},{32,48},{48,32},{64,80},{80,64},{96,112},{112,96},{1... | collective-permute-start | bytes 101768 | tf_op jit(solution)/shard_map/ppermute | solution.py:38
  107.9 7.5 %collective-permute-start.2 = (f32[8480]{0:T(1024)S(1)}, f32[8480]{0:T(1024)S(1)}, u32[]{:S(2)}, u32[]{:S(2)}) collective-permute-start(f32[8480]{0:T(1024)S(1)} %add.124), channel_id=1, source_target_pairs={{0,32},{16,48},{32,0},{48,16},{64,96},{80,112},{96,64},{112,80},{1... | collective-permute-start | bytes 101768 | tf_op jit(solution)/shard_map/ppermute | solution.py:38
  115.4 10.1 %collective-permute-start.3 = (f32[8480]{0:T(1024)S(1)}, f32[8480]{0:T(1024)S(1)}, u32[]{:S(2)}, u32[]{:S(2)}) collective-permute-start(f32[8480]{0:T(1024)S(1)} %add.125), channel_id=1, source_target_pairs={{0,64},{16,80},{32,96},{48,112},{64,0},{80,16},{96,32},{112,48},{1... | collective-permute-start | bytes 101768 | tf_op jit(solution)/shard_map/ppermute | solution.py:38
  125.5 5.8 %collective-permute-start.4 = (f32[8480]{0:T(1024)S(1)}, f32[8480]{0:T(1024)S(1)}, u32[]{:S(2)}, u32[]{:S(2)}) collective-permute-start(f32[8480]{0:T(1024)S(1)} %add.126), channel_id=1, source_target_pairs={{0,128},{16,144},{32,160},{48,176},{64,192},{80,208},{96,224},{112... | collective-permute-start | bytes 101768 | tf_op jit(solution)/shard_map/ppermute | solution.py:38
  131.4 7.3 %collective-permute-start.5 = (f32[8480]{0:T(1024)S(1)}, f32[8480]{0:T(1024)S(1)}, u32[]{:S(2)}, u32[]{:S(2)}) collective-permute-start(f32[8480]{0:T(1024)S(1)} %add.127), channel_id=1, source_target_pairs={{0,256},{16,272},{32,288},{48,304},{64,320},{80,336},{96,352},{112... | collective-permute-start | bytes 101768 | tf_op jit(solution)/shard_map/ppermute | solution.py:38
